TPU v7x, 32 devices: a whole 2x2x4 slice. The times are simulated.
32 devices in a mesh: pw: 8 (over z, y), band: 4 (over x, core).
Axes of the slice: x: 2, y: 2, z: 4, core: 2. Of those that a mesh axis runs over, the one named last changes fastest.
Arguments:
- psi_block: float32 [2, 8, 256, 128], P(None, 'band', 'pw'), may hold values from -6 to 6
- psi_all: bfloat16 [2, 1024, 256, 128], P(None, 'band', 'pw'), may hold values from -0.0234375 to 0.0234375
- potential: float32 [128, 128, 128], P('pw'), may hold values from -8 to 8
- stick_col: int32 [256], replicated, may hold values from 0 to 16383, as said below
Outputs:
- intersection: float32 [2, 8, 1024], P(None, 'pw', 'band')
- hpsi: float32 [2, 8, 256, 128], P(None, 'band', 'pw')
Inputs may be any that keep to these rules, and one draw needn't show every extreme that they name: `stick_col`: distinct columns of the 128 x 128 plane; column 0 and column 16383 are always among them.
All inputs are finite; a program needn't handle non-finite values.
Results may differ from a plain program's by a relative error of at most 0.0029.
Values may be sent and summed in bfloat16 or wider, within the bound.
No kernel may reach another device: no remote copies, remote signals or barrier semaphores. Data moves between devices by JAX's collectives and lax.ppermute only.
A program may use at most 64 MiB of HBM per device.

v0:
```python
import math
import jax
import numpy as np
import jax.numpy as jnp
from jax import lax
from jax.sharding import PartitionSpec as P


def frequency(index, size):
    return jnp.where(index < size // 2, index, index - size)


def kinetic_table(columns, grid_size):
    col_x = frequency(columns // grid_size, grid_size).astype(jnp.float32)
    col_y = frequency(columns % grid_size, grid_size).astype(jnp.float32)
    along = frequency(jnp.arange(grid_size, dtype=jnp.int32), grid_size).astype(jnp.float32)
    plane = col_x * col_x + col_y * col_y
    return 4.0 * (plane[:, None] + along[None, :] * along[None, :]) / float(grid_size * grid_size)


def dft_table(grid_size, sign):
    indices = np.arange(grid_size)
    products = indices[:, None] * indices[None, :] % grid_size
    angles = 2.0 * np.pi / grid_size * products
    cosine = np.cos(angles)
    sine = sign * np.sin(angles)
    table = np.stack([np.stack([cosine, -sine]), np.stack([sine, cosine])])
    return jnp.asarray(table.astype(np.float32))


def plane_tables(stick_col, grid_size):
    grid_iota = jnp.arange(grid_size, dtype=jnp.int32)
    col_x = stick_col // grid_size
    col_y = stick_col % grid_size
    phase_angles = (
        2.0
        * math.pi
        / grid_size
        * (grid_iota[:, None] * col_x[None, :] % grid_size).astype(jnp.float32)
    )
    place_cols = (col_y[:, None] == grid_iota[None, :]).astype(jnp.float32)
    pick_cols = (grid_iota[:, None] == col_y[None, :]).astype(jnp.float32)
    return (jnp.cos(phase_angles), jnp.sin(phase_angles), place_cols, pick_cols)


def mult(left, right):
    return jnp.dot(left, right, precision=lax.Precision.HIGH, preferred_element_type=jnp.float32)


def plane_phase(amp, pot, tables, grid_size):
    phase_cos, phase_sin, place_cols, pick_cols = tables
    inverse = dft_table(grid_size, 1.0)
    cosine = inverse[0, 0]
    sine = inverse[1, 0]
    scaled_pot = (pot / float(grid_size**3))[None]
    val_re = amp[0][:, :, None, :]
    val_im = amp[1][:, :, None, :]
    spread_re = val_re * phase_cos - val_im * phase_sin
    spread_im = val_re * phase_sin + val_im * phase_cos
    rows_re = mult(spread_re, place_cols)
    rows_im = mult(spread_im, place_cols)
    shared = mult(rows_re + rows_im, cosine)
    wave_re = (shared - mult(rows_im, cosine + sine)) * scaled_pot
    wave_im = (shared + mult(rows_re, sine - cosine)) * scaled_pot
    shared = mult(wave_re + wave_im, cosine)
    back_re = shared - mult(wave_im, cosine - sine)
    back_im = shared - mult(wave_re, sine + cosine)
    sel_re = mult(back_re, pick_cols)
    sel_im = mult(back_im, pick_cols)
    picked_re = jnp.sum(sel_re * phase_cos + sel_im * phase_sin, axis=2)
    picked_im = jnp.sum(sel_im * phase_cos - sel_re * phase_sin, axis=2)
    return jnp.stack([picked_re, picked_im])


def intersect(lowered, psi_all, pw_count):
    turned = jnp.stack([-lowered[1], lowered[0]])
    both = jnp.concatenate([lowered, turned], axis=1)
    dims = (((2, 3), (2, 3)), ((0,), (0,)))
    width = psi_all.shape[1] // 4
    partial_value = jnp.concatenate(
        [
            jnp.sum(
                lax.dot_general(
                    both,
                    psi_all[:, k * width : (k + 1) * width],
                    dims,
                    preferred_element_type=jnp.float32,
                ),
                axis=0,
            )
            for k in range(4)
        ],
        axis=-1,
    )
    partial_value = partial_value.reshape(2, lowered.shape[1], partial_value.shape[-1])
    rows_dev = partial_value.shape[1] // pw_count
    pieces = partial_value.reshape(2, pw_count, rows_dev, partial_value.shape[-1])
    pieces = lax.all_to_all(pieces, "pw", split_axis=1, concat_axis=1, tiled=True)
    return jnp.sum(pieces, axis=1)


def per_device_rows(psi_block, psi_all, potential, stick_col):
    sticks_dev = psi_block.shape[2]
    grid_size = psi_block.shape[3]
    fast = lax.Precision.HIGH
    rank = lax.axis_index("pw")
    pw_count = lax.axis_size("pw")
    planes = potential.shape[0]
    my_columns = lax.dynamic_slice_in_dim(stick_col, rank * sticks_dev, sticks_dev)
    kinetic = kinetic_table(my_columns, grid_size)
    inverse = dft_table(grid_size, 1.0)
    forward = dft_table(grid_size, -1.0)
    tables = plane_tables(stick_col, grid_size)
    parts = []
    for band in range(psi_block.shape[1]):
        coeffs = psi_block[:, band : band + 1]
        z_lines = jnp.einsum("dczk,cbsk->zdbs", inverse, coeffs, precision=fast)
        received = lax.all_to_all(z_lines, "pw", split_axis=0, concat_axis=0, tiled=True)
        lanes = received.shape[1:]
        received = received.reshape((pw_count, planes) + lanes)
        amp = jnp.transpose(received, (2, 3, 1, 0, 4)).reshape(
            lanes[0], lanes[1], planes, pw_count * sticks_dev
        )
        picked = plane_phase(amp, potential, tables, grid_size)
        outgoing = picked.reshape(lanes[0], lanes[1], planes, pw_count, sticks_dev)
        outgoing = jnp.transpose(outgoing, (3, 2, 0, 1, 4)).reshape((pw_count * planes,) + lanes)
        sticks_back = lax.all_to_all(outgoing, "pw", split_axis=0, concat_axis=0, tiled=True)
        parts.append(jnp.einsum("dckz,zcbs->dbsk", forward, sticks_back, precision=fast))
    vpsi = jnp.concatenate(parts, axis=1)
    applied = kinetic[None, None] * psi_block + vpsi
    lowered = applied.astype(jnp.bfloat16)
    gathered = lax.all_gather(lowered, "band", axis=1, tiled=True)
    intersection = intersect(gathered, psi_all, pw_count)
    return (intersection, applied)


def per_device(psi_block, psi_all, potential, stick_col):
    return per_device_rows(psi_block, psi_all, potential, stick_col)


def solution(mesh):
    return jax.shard_map(
        per_device,
        mesh=mesh,
        in_specs=(
            P(None, "band", "pw", None),
            P(None, "band", "pw", None),
            P("pw", None, None),
            P(),
        ),
        out_specs=(P(None, "pw", "band"), P(None, "band", "pw", None)),
        check_vma=False,
    )
```

profile of v0, /device:TPU:0, one launch (start us, length us, event | category | flops | bytes accessed | tf_op | source)
XLA Modules:
  0.0 94.0 jit_solution(17449898297534052666)
XLA Ops:
  0.6 1.2 %convolution_bitcast_fusion.1 = f32[128,2,1,32]{0,3,1,2:T(8,128)S(1)} fusion(f32[2,2,128,128]{3,2,1,0:T(8,128)} %constant.89.clone, f32[2,2,32,128]{3,2,1,0:T(8,128)} %param.8), kind=kOutput, calls=%fused_computation.33 | convolution fusion | flops 12582912 | bytes 327680 | tf_op jit(solution)/shard_map/dczk,cbsk->zdbs/dot_general | solution.py:117
  2.0 0.8 reshape.302
  2.7 7.3 %all-to-all-start.2 = ((f32[8,1,1024]{2,1,0:T(1,128)}), f32[8,1,1024]{2,1,0:T(1,128)S(1)}, u32[]{:S(2)}, u32[]{:S(2)}) async-start(f32[8,1,1024]{2,1,0:T(1,128)} %reshape.302), calls=%async_computation.2 | async-start | bytes 65536 | tf_op jit(solution)/shard_map/all_to_all | solution.py:118
  10.0 1.2 %convolution_bitcast_fusion.3 = f32[128,2,1,32]{0,3,1,2:T(8,128)S(1)} fusion(f32[2,2,128,128]{3,2,1,0:T(8,128)} %constant.89.clone, f32[2,2,32,128]{3,2,1,0:T(8,128)} %param.8), kind=kOutput, calls=%fused_computation.35 | convolution fusion | flops 12582912 | bytes 327680 | tf_op jit(solution)/shard_map/dczk,cbsk->zdbs/dot_general | solution.py:117
  12.6 0.8 reshape.300
  13.4 4.1 %fusion.88 = (bf16[2,64,32,128]{3,2,1,0:T(8,128)(2,1)}, bf16[2,64,32,128]{3,2,1,0:T(8,128)(2,1)}, bf16[2,64,32,128]{3,2,1,0:T(8,128)(2,1)}, bf16[2,64,32,128]{3,2,1,0:T(8,128)(2,1)S(1)}) fusion(bf16[2,256,32,128]{3,2,1,0:T(8,128)(2,1)} %param.9), kind=kLoop, calls=%fused_computation.129 | loop fusion | bytes 8388608 | tf_op jit(solution)/shard_map/slice | solution.py:85
  17.6 6.0 %all-to-all-start = ((f32[8,1,1024]{2,1,0:T(1,128)}), f32[8,1,1024]{2,1,0:T(1,128)S(1)}, u32[]{:S(2)}, u32[]{:S(2)}) async-start(f32[8,1,1024]{2,1,0:T(1,128)} %reshape.300), calls=%async_computation | async-start | bytes 65536 | tf_op jit(solution)/shard_map/all_to_all | solution.py:118
  24.1 0.7 reduce.10
  25.3 0.8 fusion
  26.1 0.8 fusion.4
  26.9 3.4 %all-to-all-done = f32[8,1,1024]{2,1,0:T(1,128)S(1)} async-done(((f32[8,1,1024]{2,1,0:T(1,128)}), f32[8,1,1024]{2,1,0:T(1,128)S(1)}, u32[]{:S(2)}, u32[]{:S(2)}) %all-to-all-start) | async-done | bytes 32800 | tf_op jit(solution)/shard_map/all_to_all | solution.py:118
  30.3 0.7 reduce.9
  31.5 1.7 %fusion.12 = f32[16,128,128]{2,1,0:T(8,128)S(1)} fusion(f32[128,256]{1,0:T(8,128)} %copy-done.9, f32[16,256]{1,0:T(8,128)S(1)} %mul.266, f32[128,256]{1,0:T(8,128)S(1)} %get-tuple-element.30, f32[16,256]{1,0:T(8,128)S(1)} %mul.257, s32[256]{0:T(256)S(1)} %get-tuple-element.28), kind=kOutput, calls=%fused_computation.16 | convolution fusion | flops 404258816 | bytes 1344512 | tf_op jit(solution)/shard_map/dot_general | solution.py:47
  33.2 1.7 %fusion.8 = f32[16,128,128]{2,1,0:T(8,128)S(1)} fusion(f32[128,256]{1,0:T(8,128)} %copy-done.9, f32[16,256]{1,0:T(8,128)S(1)} %mul.266, f32[128,256]{1,0:T(8,128)S(1)} %get-tuple-element.30, f32[16,256]{1,0:T(8,128)S(1)} %mul.257, s32[256]{0:T(256)S(1)} %get-tuple-element.28), kind=kOutput, calls=%fused_computation.12 | convolution fusion | flops 404258816 | bytes 1344512 | tf_op jit(solution)/shard_map/dot_general | solution.py:47
  44.4 0.9 fusion.66
  45.3 1.7 %add_reduce_fusion.1 = (f32[16,256]{1,0:T(8,128)S(1)}, f32[16,256]{1,0:T(8,128)S(1)}, f32[16,256]{1,0:T(8,128)S(1)}, f32[16,256]{1,0:T(8,128)S(1)}) fusion(f32[16,128,256]{2,1,0:T(8,128)S(1)} %fusion.66, f32[128,256]{1,0:T(8,128)S(1)} %copy-done.10, f32[128,256]{1,0:T(8,128)S(1)} %get-tuple-element.30, f32[16,128,256]{2,1,0:T(8,128)S(1)} %fusion.62, ...), kind=kOutput, calls=%fused_computation.11 | convolution fusion | flops 411058176 | bytes 7668736 | tf_op jit(solution)/shard_map/dot_general | solution.py:47
  47.3 0.8 reshape.306
  48.1 3.3 %all-to-all-start.1 = ((f32[8,1,1024]{2,1,0:T(1,128)}), f32[8,1,1024]{2,1,0:T(1,128)S(1)}, u32[]{:S(2)}, u32[]{:S(2)}) async-start(f32[8,1,1024]{2,1,0:T(1,128)} %reshape.306), calls=%async_computation.1 | async-start | bytes 65536 | tf_op jit(solution)/shard_map/all_to_all | solution.py:127
  51.8 0.8 reshape.304
  52.5 5.5 %all-to-all-done.1 = f32[8,1,1024]{2,1,0:T(1,128)S(1)} async-done(((f32[8,1,1024]{2,1,0:T(1,128)}), f32[8,1,1024]{2,1,0:T(1,128)S(1)}, u32[]{:S(2)}, u32[]{:S(2)}) %all-to-all-start.1) | async-done | bytes 32800 | tf_op jit(solution)/shard_map/all_to_all | solution.py:127
  58.1 4.0 %all-to-all-start.3 = ((f32[8,1,1024]{2,1,0:T(1,128)}), f32[8,1,1024]{2,1,0:T(1,128)}, u32[]{:S(2)}, u32[]{:S(2)}) async-start(f32[8,1,1024]{2,1,0:T(1,128)} %reshape.304), calls=%async_computation.3 | async-start | bytes 65536 | tf_op jit(solution)/shard_map/all_to_all | solution.py:127
  62.1 1.4 %reduce.12 = f32[8,1024]{1,0:T(8,128)} reduce(f32[8,1,1024]{2,1,0:T(1,128)S(1)} %all-to-all-done.1, f32[]{:T(128)} %broadcast.248), dimensions={1}, to_apply=%all_to_all.16.reduce_sub_computation | reduce | bytes 65540 | tf_op jit(solution)/shard_map/all_to_all | solution.py:127
  63.5 0.9 reshape.307
  65.1 3.6 %all-to-all-done.3 = f32[8,1,1024]{2,1,0:T(1,128)} async-done(((f32[8,1,1024]{2,1,0:T(1,128)}), f32[8,1,1024]{2,1,0:T(1,128)}, u32[]{:S(2)}, u32[]{:S(2)}) %all-to-all-start.3) | async-done | bytes 32800 | tf_op jit(solution)/shard_map/all_to_all | solution.py:127
  68.7 2.1 %reduce.11 = f32[8,1024]{1,0:T(8,128)} reduce(f32[8,1,1024]{2,1,0:T(1,128)} %all-to-all-done.3, f32[]{:T(128)} %broadcast.248), dimensions={1}, to_apply=%all_to_all.18.reduce_sub_computation | reduce | bytes 65540 | tf_op jit(solution)/shard_map/all_to_all | solution.py:127
  70.8 0.9 reshape.305
  72.5 1.0 %convolution_bitcast_fusion.2 = f32[2,1,32,128]{3,2,0,1:T(8,128)S(1)} fusion(f32[2,2,128,128]{3,2,1,0:T(8,128)S(1)} %copy-done.3, f32[128,2,1,32]{0,3,1,2:T(8,128)} %copy.74), kind=kOutput, calls=%fused_computation.34 | convolution fusion | flops 12582912 | bytes 327680 | tf_op jit(solution)/shard_map/dckz,zcbs->dbsk/dot_general | solution.py:128
  73.5 1.0 %convolution_bitcast_fusion = f32[2,1,32,128]{3,2,0,1:T(8,128)S(1)} fusion(f32[2,2,128,128]{3,2,1,0:T(8,128)S(1)} %copy-done.3, f32[128,2,1,32]{0,3,1,2:T(8,128)} %copy.82), kind=kOutput, calls=%fused_computation.32 | convolution fusion | flops 12582912 | bytes 327680 | tf_op jit(solution)/shard_map/dckz,zcbs->dbsk/dot_general | solution.py:128
  74.5 0.9 fusion.87
  75.4 5.4 %all_gather.3 = bf16[2,8,32,128]{3,2,0,1:T(8,128)(2,1)S(1)} all-gather(bf16[2,2,32,128]{3,2,0,1:T(8,128)(2,1)S(1)} %get-tuple-element.16), channel_id=1, replica_groups=mesh['pw'=8,'band'=4] {'band'}, dimensions={1}, use_global_device_ids=true | all-gather | bytes 163840 | tf_op jit(solution)/shard_map/all_gather | solution.py:132
  83.6 3.3 %all-to-all-start.4 = ((f32[2,8,1,256]{3,0,2,1:T(2,128)}), f32[2,8,1,256]{3,0,2,1:T(2,128)S(1)}, u32[]{:S(2)}, u32[]{:S(2)}) async-start(f32[2,8,1,256]{3,0,2,1:T(2,128)} %copy.90), calls=%async_computation.4 | async-start | bytes 32768 | tf_op jit(solution)/shard_map/all_to_all | solution.py:98
  87.5 5.9 %all-to-all-done.4 = f32[2,8,1,256]{3,0,2,1:T(2,128)S(1)} async-done(((f32[2,8,1,256]{3,0,2,1:T(2,128)}), f32[2,8,1,256]{3,0,2,1:T(2,128)S(1)}, u32[]{:S(2)}, u32[]{:S(2)}) %all-to-all-start.4) | async-done | bytes 16416 | tf_op jit(solution)/shard_map/all_to_all | solution.py:98
  (84 shorter events, 18.3 us)
Async XLA Ops:
  2.7 14.9 %all-to-all-start.2 = ((f32[8,1,1024]{2,1,0:T(1,128)}), f32[8,1,1024]{2,1,0:T(1,128)S(1)}, u32[]{:S(2)}, u32[]{:S(2)}) async-start(f32[8,1,1024]{2,1,0:T(1,128)} %reshape.302), calls=%async_computation.2 | async-start | bytes 65536 | tf_op jit(solution)/shard_map/all_to_all | solution.py:118
  12.5 13.6 %copy-start.9 = (f32[128,256]{1,0:T(8,128)}, f32[128,256]{1,0:T(8,128)S(1)}, u32[]{:S(2)}) copy-start(f32[128,256]{1,0:T(8,128)S(1)} %get-tuple-element.31) | copy-start | bytes 393220
  13.4 4.1 %copy-start.11 = (s32[256]{0:T(256)S(1)}, s32[256]{0:T(256)}, u32[]{:S(2)}) copy-start(s32[256]{0:T(256)} %param.11) | copy-start | bytes 3076
  17.6 12.7 %all-to-all-start = ((f32[8,1,1024]{2,1,0:T(1,128)}), f32[8,1,1024]{2,1,0:T(1,128)S(1)}, u32[]{:S(2)}, u32[]{:S(2)}) async-start(f32[8,1,1024]{2,1,0:T(1,128)} %reshape.300), calls=%async_computation | async-start | bytes 65536 | tf_op jit(solution)/shard_map/all_to_all | solution.py:118
  31.3 3.5 %copy-start.2 = (f32[128,128,1]{1,0,2:T(8,128)S(1)}, f32[128,128,1]{1,0,2:T(8,128)}, u32[]{:S(2)}) copy-start(f32[128,128,1]{1,0,2:T(8,128)} %constant.101) | copy-start | bytes 196612
  34.9 1.2 %copy-start = (f32[16,128,128]{2,1,0:T(8,128)S(1)}, f32[16,128,128]{2,1,0:T(8,128)}, u32[]{:S(2)}) copy-start(f32[16,128,128]{2,1,0:T(8,128)} %param.10) | copy-start | bytes 3145732
  34.9 1.2 %copy-start.7 = (f32[128,128,1]{1,0,2:T(8,128)S(1)}, f32[128,128,1]{1,0,2:T(8,128)}, u32[]{:S(2)}) copy-start(f32[128,128,1]{1,0,2:T(8,128)} %constant.103) | copy-start | bytes 196612
  36.1 0.8 copy-start.1
  39.8 0.8 copy-start.8
  44.4 0.9 copy-start.10
  47.0 25.4 %copy-start.3 = (f32[2,2,128,128]{3,2,1,0:T(8,128)S(1)}, f32[2,2,128,128]{3,2,1,0:T(8,128)}, u32[]{:S(2)}) copy-start(f32[2,2,128,128]{3,2,1,0:T(8,128)} %constant.90.clone) | copy-start | bytes 786436
  47.2 33.7 %copy-start.6 = (bf16[2,64,32,128]{3,2,1,0:T(8,128)(2,1)S(1)}, bf16[2,64,32,128]{3,2,1,0:T(8,128)(2,1)}, u32[]{:S(2)}) copy-start(bf16[2,64,32,128]{3,2,1,0:T(8,128)(2,1)} %get-tuple-element.18) | copy-start | bytes 3145732
  48.1 10.0 %all-to-all-start.1 = ((f32[8,1,1024]{2,1,0:T(1,128)}), f32[8,1,1024]{2,1,0:T(1,128)S(1)}, u32[]{:S(2)}, u32[]{:S(2)}) async-start(f32[8,1,1024]{2,1,0:T(1,128)} %reshape.306), calls=%async_computation.1 | async-start | bytes 65536 | tf_op jit(solution)/shard_map/all_to_all | solution.py:127
  58.1 10.7 %all-to-all-start.3 = ((f32[8,1,1024]{2,1,0:T(1,128)}), f32[8,1,1024]{2,1,0:T(1,128)}, u32[]{:S(2)}, u32[]{:S(2)}) async-start(f32[8,1,1024]{2,1,0:T(1,128)} %reshape.304), calls=%async_computation.3 | async-start | bytes 65536 | tf_op jit(solution)/shard_map/all_to_all | solution.py:127
  62.1 19.2 %copy-start.5 = (bf16[2,64,32,128]{3,2,1,0:T(8,128)(2,1)S(1)}, bf16[2,64,32,128]{3,2,1,0:T(8,128)(2,1)}, u32[]{:S(2)}) copy-start(bf16[2,64,32,128]{3,2,1,0:T(8,128)(2,1)} %get-tuple-element.20) | copy-start | bytes 3145732
  80.8 1.2 %copy-start.4 = (bf16[2,64,32,128]{3,2,1,0:T(8,128)(2,1)S(1)}, bf16[2,64,32,128]{3,2,1,0:T(8,128)(2,1)}, u32[]{:S(2)}) copy-start(bf16[2,64,32,128]{3,2,1,0:T(8,128)(2,1)} %get-tuple-element.19) | copy-start | bytes 3145732
  83.6 9.8 %all-to-all-start.4 = ((f32[2,8,1,256]{3,0,2,1:T(2,128)}), f32[2,8,1,256]{3,0,2,1:T(2,128)S(1)}, u32[]{:S(2)}, u32[]{:S(2)}) async-start(f32[2,8,1,256]{3,0,2,1:T(2,128)} %copy.90), calls=%async_computation.4 | async-start | bytes 32768 | tf_op jit(solution)/shard_map/all_to_all | solution.py:98
where the time goes:
time: 95.2 us; the launch traced here: 94 us
  starting transfers between devices  23.9 us (25%)
  matrix products  22 us (23%)
  waiting for transfers between devices  18.4 us (19%)
  local copies, waits for them, and re-layouts  15.8 us (17%)
  other arithmetic  7.35 us (8%)
  blocking collectives  5.43 us (6%)
  between operations  1.15 us (1%)
    dot_general x20, matrix products, mult(): jnp.dot(left, right, precision=lax.Precision.HIGH, preferred_element_type...  15.8 us
    all_to_all x2, starting transfers between devices, per_device_rows(): lax.all_to_all(z_lines, 'pw', split_axis=0, concat_axis=0, tiled=True)  13.3 us
    all_to_all x2, waiting for transfers between devices, per_device_rows(): lax.all_to_all(outgoing, 'pw', split_axis=0, concat_axis=0, tiled=True)  9.14 us
    all_to_all x2, starting transfers between devices, per_device_rows(): lax.all_to_all(outgoing, 'pw', split_axis=0, concat_axis=0, tiled=True)  7.3 us
    unnamed x33, local copies, waits for them, and re-layouts  7.24 us
    all_to_all x1, waiting for transfers between devices, intersect(): lax.all_to_all(pieces, 'pw', split_axis=1, concat_axis=1, tiled=True)  5.88 us
    all_gather x1, blocking collectives, per_device_rows(): gathered = lax.all_gather(lowered, 'band', axis=1, tiled=True)  5.43 us
    slice x1, local copies, waits for them, and re-layouts, intersect(): psi_all[:, k * width:(k + 1) * width]  4.12 us
  transfers between devices with their start and end apart: 5, of which 4 were waited for; matrix products, arithmetic and copies ran while one was open for 17% of the time, Pallas kernels for 0%

commit v1 on v0

--- a/solution.py
+++ b/solution.py
@@ -4,6 +4,18 @@
 import jax.numpy as jnp
 from jax import lax
 from jax.sharding import PartitionSpec as P
+
+
+def collect(x, axis, dim):
+    ways, here = (lax.axis_size(axis), lax.axis_index(axis))
+    grown, reach = (x, 1)
+    while reach < ways:
+        theirs = lax.ppermute(grown, axis, [(d, d ^ reach) for d in range(ways)])
+        mine_first = jnp.concatenate([grown, theirs], axis=dim)
+        theirs_first = jnp.concatenate([theirs, grown], axis=dim)
+        grown = jnp.where(here & reach == 0, mine_first, theirs_first)
+        reach = 2 * reach
+    return grown
 
 
 def frequency(index, size):
@@ -129,7 +141,7 @@
     vpsi = jnp.concatenate(parts, axis=1)
     applied = kinetic[None, None] * psi_block + vpsi
     lowered = applied.astype(jnp.bfloat16)
-    gathered = lax.all_gather(lowered, "band", axis=1, tiled=True)
+    gathered = collect(lowered, "band", 1)
     intersection = intersect(gathered, psi_all, pw_count)
     return (intersection, applied)
 

time: 95.2 us -> 86.6 us (0.910)
  waiting for transfers between devices: 18.4 us -> 24.2 us
  blocking collectives: 5.43 us -> 0 us
  local copies, waits for them, and re-layouts: 15.8 us -> 12.7 us
  other arithmetic: 7.35 us -> 5.17 us
  matrix products: 22 us -> 20.3 us
  starting transfers between devices: 23.9 us -> 22.4 us
    all_gather x1 -> x0, blocking collectives: 5.43 us -> none  [per_device_rows(): gathered = lax.all_gather(lowered, 'band', axis=1, tiled=True)]
    all_to_all x2, waiting for transfers between devices: 3.41 us -> 5.99 us  [per_device_rows(): lax.all_to_all(z_lines, 'pw', split_axis=0, concat_axis=0, tiled=True)]
    all_to_all x2, starting transfers between devices: 13.3 us -> 10.7 us  [per_device_rows(): lax.all_to_all(z_lines, 'pw', split_axis=0, concat_axis=0, tiled=True)]
    all_to_all x2, other arithmetic: 3.5 us -> 1.44 us  [per_device_rows(): lax.all_to_all(outgoing, 'pw', split_axis=0, concat_axis=0, tiled=True)]
    all_to_all x2, waiting for transfers between devices: 9.14 us -> 11.1 us  [per_device_rows(): lax.all_to_all(outgoing, 'pw', split_axis=0, concat_axis=0, tiled=True)]
    dot_general x20, matrix products: 15.8 us -> 14 us  [mult(): jnp.dot(left, right, precision=lax.Precision.HIGH, preferred_element_type...]
    unnamed x33 -> x23, local copies, waits for them, and re-layouts: 7.24 us -> 5.52 us
    dot_general x4, matrix products: 1.72 us -> 3.38 us  [intersect(): lax.dot_general(both, psi_all[:, k * width:(k + 1) * width], dims, prefer...]
  transfers between devices with their start and end apart: 5 -> 7, of which waited for: 4 -> 6; matrix products, arithmetic and copies ran while one was open for 17% -> 16% of each run, Pallas kernels for 0% -> 0%
where the time goes in v1:
time: 86.6 us; the launch traced here: 85.9 us
  waiting for transfers between devices  24.2 us (28%)
  starting transfers between devices  22.4 us (26%)
  matrix products  20.3 us (23%)
  local copies, waits for them, and re-layouts  12.7 us (15%)
  other arithmetic  5.17 us (6%)
  between operations  1.16 us (1%)
    dot_general x20, matrix products, mult(): jnp.dot(left, right, precision=lax.Precision.HIGH, preferred_element_type...  14 us
    all_to_all x2, waiting for transfers between devices, per_device_rows(): lax.all_to_all(outgoing, 'pw', split_axis=0, concat_axis=0, tiled=True)  11.1 us
    all_to_all x2, starting transfers between devices, per_device_rows(): lax.all_to_all(z_lines, 'pw', split_axis=0, concat_axis=0, tiled=True)  10.7 us
    all_to_all x2, starting transfers between devices, per_device_rows(): lax.all_to_all(outgoing, 'pw', split_axis=0, concat_axis=0, tiled=True)  6.67 us
    all_to_all x2, waiting for transfers between devices, per_device_rows(): lax.all_to_all(z_lines, 'pw', split_axis=0, concat_axis=0, tiled=True)  5.99 us
    all_to_all x1, waiting for transfers between devices, intersect(): lax.all_to_all(pieces, 'pw', split_axis=1, concat_axis=1, tiled=True)  5.88 us
    unnamed x23, local copies, waits for them, and re-layouts  5.52 us
    slice x1, local copies, waits for them, and re-layouts, intersect(): psi_all[:, k * width:(k + 1) * width]  4.06 us
  transfers between devices with their start and end apart: 7, of which 6 were waited for; matrix products, arithmetic and copies ran while one was open for 16% of the time, Pallas kernels for 0%

profile of v1, /device:TPU:0, one launch (start us, length us, event | category | flops | bytes accessed | tf_op | source)
XLA Modules:
  0.0 85.9 jit_solution(2463559125410159299)
XLA Ops:
  0.6 1.2 %convolution_bitcast_fusion.1 = f32[128,2,1,32]{0,3,1,2:T(8,128)S(1)} fusion(f32[2,2,128,128]{3,2,1,0:T(8,128)} %constant.95.clone, f32[2,2,32,128]{3,2,1,0:T(8,128)} %param.8), kind=kOutput, calls=%fused_computation.33 | convolution fusion | flops 12582912 | bytes 327680 | tf_op jit(solution)/shard_map/dczk,cbsk->zdbs/dot_general | solution.py:129
  2.0 0.8 reshape.302
  2.7 7.3 %all-to-all-start.2 = ((f32[8,1,1024]{2,1,0:T(1,128)}), f32[8,1,1024]{2,1,0:T(1,128)S(1)}, u32[]{:S(2)}, u32[]{:S(2)}) async-start(f32[8,1,1024]{2,1,0:T(1,128)} %reshape.302), calls=%async_computation.2 | async-start | bytes 65536 | tf_op jit(solution)/shard_map/all_to_all | solution.py:130
  10.0 1.2 %convolution_bitcast_fusion.3 = f32[128,2,1,32]{0,3,1,2:T(8,128)S(1)} fusion(f32[2,2,128,128]{3,2,1,0:T(8,128)} %constant.95.clone, f32[2,2,32,128]{3,2,1,0:T(8,128)} %param.8), kind=kOutput, calls=%fused_computation.35 | convolution fusion | flops 12582912 | bytes 327680 | tf_op jit(solution)/shard_map/dczk,cbsk->zdbs/dot_general | solution.py:129
  12.6 0.8 reshape.300
  13.4 0.8 fusion.86
  14.1 2.6 %all-to-all-done.2 = f32[8,1,1024]{2,1,0:T(1,128)S(1)} async-done(((f32[8,1,1024]{2,1,0:T(1,128)}), f32[8,1,1024]{2,1,0:T(1,128)S(1)}, u32[]{:S(2)}, u32[]{:S(2)}) %all-to-all-start.2) | async-done | bytes 32800 | tf_op jit(solution)/shard_map/all_to_all | solution.py:130
  16.7 3.4 %all-to-all-start = ((f32[8,1,1024]{2,1,0:T(1,128)}), f32[8,1,1024]{2,1,0:T(1,128)S(1)}, u32[]{:S(2)}, u32[]{:S(2)}) async-start(f32[8,1,1024]{2,1,0:T(1,128)} %reshape.300), calls=%async_computation | async-start | bytes 65536 | tf_op jit(solution)/shard_map/all_to_all | solution.py:130
  20.7 0.7 reduce.10
  21.8 0.8 fusion
  22.6 0.8 fusion.4
  23.4 3.4 %all-to-all-done = f32[8,1,1024]{2,1,0:T(1,128)S(1)} async-done(((f32[8,1,1024]{2,1,0:T(1,128)}), f32[8,1,1024]{2,1,0:T(1,128)S(1)}, u32[]{:S(2)}, u32[]{:S(2)}) %all-to-all-start) | async-done | bytes 32800 | tf_op jit(solution)/shard_map/all_to_all | solution.py:130
  26.8 0.7 reduce.9
  28.0 0.8 fusion.12
  28.8 0.8 fusion.8
  38.4 0.7 fusion.66
  39.2 0.9 %fusion.70 = f32[16,128,256]{2,1,0:T(8,128)S(1)} fusion(f32[16,128,128]{2,1,0:T(8,128)S(1)} %convolution_subtract_fusion.4, s32[256]{0:T(256)S(1)} %get-tuple-element.28), kind=kOutput, calls=%fused_computation.92 | convolution fusion | flops 402685952 | bytes 3146752 | tf_op jit(solution)/shard_map/dot_general | solution.py:59
  40.1 1.6 %add_reduce_fusion.1 = (f32[16,256]{1,0:T(8,128)S(1)}, f32[16,256]{1,0:T(8,128)S(1)}, f32[16,256]{1,0:T(8,128)S(1)}, f32[16,256]{1,0:T(8,128)S(1)}) fusion(f32[16,128,256]{2,1,0:T(8,128)S(1)} %fusion.70, f32[128,256]{1,0:T(8,128)S(1)} %get-tuple-element.31, f32[128,256]{1,0:T(8,128)S(1)} %get-tuple-element.30, f32[16,128,256]{2,1,0:T(8,128)S(1)} %fusion.66, ...), kind=kOutput, calls=%fused_computation.11 | convolution fusion | flops 411058176 | bytes 7668736 | tf_op jit(solution)/shard_map/dot_general | solution.py:59
  42.1 0.8 reshape.306
  42.8 3.3 %all-to-all-start.1 = ((f32[8,1,1024]{2,1,0:T(1,128)}), f32[8,1,1024]{2,1,0:T(1,128)S(1)}, u32[]{:S(2)}, u32[]{:S(2)}) async-start(f32[8,1,1024]{2,1,0:T(1,128)} %reshape.306), calls=%async_computation.1 | async-start | bytes 65536 | tf_op jit(solution)/shard_map/all_to_all | solution.py:139
  46.5 0.8 reshape.304
  47.3 5.5 %all-to-all-done.1 = f32[8,1,1024]{2,1,0:T(1,128)S(1)} async-done(((f32[8,1,1024]{2,1,0:T(1,128)}), f32[8,1,1024]{2,1,0:T(1,128)S(1)}, u32[]{:S(2)}, u32[]{:S(2)}) %all-to-all-start.1) | async-done | bytes 32800 | tf_op jit(solution)/shard_map/all_to_all | solution.py:139
  52.8 3.3 %all-to-all-start.3 = ((f32[8,1,1024]{2,1,0:T(1,128)}), f32[8,1,1024]{2,1,0:T(1,128)S(1)}, u32[]{:S(2)}, u32[]{:S(2)}) async-start(f32[8,1,1024]{2,1,0:T(1,128)} %reshape.304), calls=%async_computation.3 | async-start | bytes 65536 | tf_op jit(solution)/shard_map/all_to_all | solution.py:139
  56.2 0.7 reduce.12
  57.2 5.6 %all-to-all-done.3 = f32[8,1,1024]{2,1,0:T(1,128)S(1)} async-done(((f32[8,1,1024]{2,1,0:T(1,128)}), f32[8,1,1024]{2,1,0:T(1,128)S(1)}, u32[]{:S(2)}, u32[]{:S(2)}) %all-to-all-start.3) | async-done | bytes 32800 | tf_op jit(solution)/shard_map/all_to_all | solution.py:139
  62.8 0.7 reduce.11
  64.4 1.2 %collective-permute-done = bf16[2,2,32,128]{3,2,0,1:T(8,128)(2,1)S(1)} collective-permute-done((bf16[2,2,32,128]{3,2,0,1:T(8,128)(2,1)S(1)}, bf16[2,2,32,128]{3,2,0,1:T(8,128)(2,1)S(1)}, u32[]{:S(2)}, u32[]{:S(2)}) %collective-permute-start) | collective-permute-done | bytes 32800 | tf_op jit(solution)/shard_map/ppermute | solution.py:13
  65.6 1.6 %collective-permute-start.1 = (bf16[2,4,32,128]{3,2,0,1:T(8,128)(2,1)S(1)}, bf16[2,4,32,128]{3,2,0,1:T(8,128)(2,1)S(1)}, u32[]{:S(2)}, u32[]{:S(2)}) collective-permute-start(bf16[2,4,32,128]{3,2,0,1:T(8,128)(2,1)S(1)} %maximum_select_fusion.1), channel_id=1, source_target_pairs={{0,2},{1,3},{2,0},{3,1},{4,6},{5,7},{6,4},{7,5},{8,10},{9,11},{10,... | collective-permute-start | bytes 196616 | tf_op jit(solution)/shard_map/ppermute | solution.py:13
  67.2 4.1 %fusion.92 = (bf16[2,64,32,128]{3,2,1,0:T(8,128)(2,1)}, bf16[2,64,32,128]{3,2,1,0:T(8,128)(2,1)S(1)}, bf16[2,64,32,128]{3,2,1,0:T(8,128)(2,1)S(1)}, bf16[2,64,32,128]{3,2,1,0:T(8,128)(2,1)S(1)}) fusion(bf16[2,256,32,128]{3,2,1,0:T(8,128)(2,1)} %param.9), kind=kLoop, calls=%fused_computation.135 | loop fusion | bytes 8388608 | tf_op jit(solution)/shard_map/slice | solution.py:97
  71.3 1.8 %convolution_bitcast_fusion.7 = f32[16,64]{1,0:T(8,128)S(1)} fusion(bf16[2,64,32,128]{3,2,1,0:T(8,128)(2,1)} %get-tuple-element.18, bf16[2,16,32,128]{3,2,0,1:T(8,128)(2,1)S(1)} %maximum_maximum_fusion), kind=kOutput, calls=%fused_computation.39 | convolution fusion | flops 16777216 | bytes 1314816 | tf_op jit(solution)/shard_map/dot_general | solution.py:95
  75.4 3.3 %all-to-all-start.4 = ((f32[2,8,1,256]{3,0,2,1:T(2,128)}), f32[2,8,1,256]{3,0,2,1:T(2,128)S(1)}, u32[]{:S(2)}, u32[]{:S(2)}) async-start(f32[2,8,1,256]{3,0,2,1:T(2,128)} %copy.91), calls=%async_computation.4 | async-start | bytes 32768 | tf_op jit(solution)/shard_map/all_to_all | solution.py:110
  79.4 5.9 %all-to-all-done.4 = f32[2,8,1,256]{3,0,2,1:T(2,128)S(1)} async-done(((f32[2,8,1,256]{3,0,2,1:T(2,128)}), f32[2,8,1,256]{3,0,2,1:T(2,128)S(1)}, u32[]{:S(2)}, u32[]{:S(2)}) %all-to-all-start.4) | async-done | bytes 16416 | tf_op jit(solution)/shard_map/all_to_all | solution.py:110
  (79 shorter events, 16.8 us)
Async XLA Ops:
  2.7 14.0 %all-to-all-start.2 = ((f32[8,1,1024]{2,1,0:T(1,128)}), f32[8,1,1024]{2,1,0:T(1,128)S(1)}, u32[]{:S(2)}, u32[]{:S(2)}) async-start(f32[8,1,1024]{2,1,0:T(1,128)} %reshape.302), calls=%async_computation.2 | async-start | bytes 65536 | tf_op jit(solution)/shard_map/all_to_all | solution.py:130
  16.7 10.1 %all-to-all-start = ((f32[8,1,1024]{2,1,0:T(1,128)}), f32[8,1,1024]{2,1,0:T(1,128)S(1)}, u32[]{:S(2)}, u32[]{:S(2)}) async-start(f32[8,1,1024]{2,1,0:T(1,128)} %reshape.300), calls=%async_computation | async-start | bytes 65536 | tf_op jit(solution)/shard_map/all_to_all | solution.py:130
  27.9 1.7 %copy-start.2 = (f32[128,128,1]{1,0,2:T(8,128)S(1)}, f32[128,128,1]{1,0,2:T(8,128)}, u32[]{:S(2)}) copy-start(f32[128,128,1]{1,0,2:T(8,128)} %constant.107) | copy-start | bytes 196612
  29.6 1.2 %copy-start = (f32[16,128,128]{2,1,0:T(8,128)S(1)}, f32[16,128,128]{2,1,0:T(8,128)}, u32[]{:S(2)}) copy-start(f32[16,128,128]{2,1,0:T(8,128)} %param.10) | copy-start | bytes 3145732
  29.6 1.2 %copy-start.4 = (f32[128,128,1]{1,0,2:T(8,128)S(1)}, f32[128,128,1]{1,0,2:T(8,128)}, u32[]{:S(2)}) copy-start(f32[128,128,1]{1,0,2:T(8,128)} %constant.109) | copy-start | bytes 196612
  30.8 0.8 copy-start.1
  34.6 0.8 copy-start.5
  41.7 22.0 %copy-start.3 = (f32[2,2,128,128]{3,2,1,0:T(8,128)S(1)}, f32[2,2,128,128]{3,2,1,0:T(8,128)}, u32[]{:S(2)}) copy-start(f32[2,2,128,128]{3,2,1,0:T(8,128)} %constant.96.clone) | copy-start | bytes 786436
  41.7 22.6 %copy-start.6 = (f32[2,2,32,128]{3,2,1,0:T(8,128)S(1)}, f32[2,2,32,128]{3,2,1,0:T(8,128)}, u32[]{:S(2)}) copy-start(f32[2,2,32,128]{3,2,1,0:T(8,128)} %param.8) | copy-start | bytes 196612
  42.8 10.0 %all-to-all-start.1 = ((f32[8,1,1024]{2,1,0:T(1,128)}), f32[8,1,1024]{2,1,0:T(1,128)S(1)}, u32[]{:S(2)}, u32[]{:S(2)}) async-start(f32[8,1,1024]{2,1,0:T(1,128)} %reshape.306), calls=%async_computation.1 | async-start | bytes 65536 | tf_op jit(solution)/shard_map/all_to_all | solution.py:139
  52.8 10.0 %all-to-all-start.3 = ((f32[8,1,1024]{2,1,0:T(1,128)}), f32[8,1,1024]{2,1,0:T(1,128)S(1)}, u32[]{:S(2)}, u32[]{:S(2)}) async-start(f32[8,1,1024]{2,1,0:T(1,128)} %reshape.304), calls=%async_computation.3 | async-start | bytes 65536 | tf_op jit(solution)/shard_map/all_to_all | solution.py:139
  64.3 1.3 %collective-permute-start = (bf16[2,2,32,128]{3,2,0,1:T(8,128)(2,1)S(1)}, bf16[2,2,32,128]{3,2,0,1:T(8,128)(2,1)S(1)}, u32[]{:S(2)}, u32[]{:S(2)}) collective-permute-start(bf16[2,2,32,128]{3,2,0,1:T(8,128)(2,1)S(1)} %get-tuple-element.16), channel_id=1, source_target_pairs={{0,1},{1,0},{2,3},{3,2},{4,5},{5,4},{6,7},{7,6},{8,9},{9,8},{10,11... | collective-permute-start | bytes 98312 | tf_op jit(solution)/shard_map/ppermute | solution.py:13
  65.6 5.6 %collective-permute-start.1 = (bf16[2,4,32,128]{3,2,0,1:T(8,128)(2,1)S(1)}, bf16[2,4,32,128]{3,2,0,1:T(8,128)(2,1)S(1)}, u32[]{:S(2)}, u32[]{:S(2)}) collective-permute-start(bf16[2,4,32,128]{3,2,0,1:T(8,128)(2,1)S(1)} %maximum_select_fusion.1), channel_id=1, source_target_pairs={{0,2},{1,3},{2,0},{3,1},{4,6},{5,7},{6,4},{7,5},{8,10},{9,11},{10,... | collective-permute-start | bytes 196616 | tf_op jit(solution)/shard_map/ppermute | solution.py:13
  75.4 9.8 %all-to-all-start.4 = ((f32[2,8,1,256]{3,0,2,1:T(2,128)}), f32[2,8,1,256]{3,0,2,1:T(2,128)S(1)}, u32[]{:S(2)}, u32[]{:S(2)}) async-start(f32[2,8,1,256]{3,0,2,1:T(2,128)} %copy.91), calls=%async_computation.4 | async-start | bytes 32768 | tf_op jit(solution)/shard_map/all_to_all | solution.py:110
